TPU v7x, 256 devices: a whole 4x4x8 slice. The times are simulated.
256 devices in a mesh: row: 16 (over z, y_hi), col: 16 (over x, y_lo, core).
Axes of the slice: x: 4, y: 4 (y_hi: 2, y_lo: 2; y = y_hi * 2 + y_lo), z: 8, core: 2. Of those that a mesh axis runs over, the one named last changes fastest.
Arguments:
- queries: bfloat16 [32, 2048, 128], P('row', 'col'), may hold values from -6.5 to 6.5
- keys: bfloat16 [32, 2048, 128], P('row', 'col'), may hold values from -6.5 to 6.5
- values: bfloat16 [32, 2048, 128], P('row', 'col'), may hold values from -6 to 6
- gate: bfloat16 [32, 2048, 128], P('row', 'col'), may hold values from -6 to 6
- bias: bfloat16 [4, 2048, 2048], P(None, 'col'), may hold values from -7.5 to 7.5
- grad_out: bfloat16 [32, 2048, 128], P('row', 'col'), may hold values from -6 to 6
- block_mask: int32 [16, 16], replicated, may hold values from 0 to 1, as said below
Outputs:
- query_grad: bfloat16 [32, 2048, 128], P('row', 'col')
- key_grad: bfloat16 [32, 2048, 128], P('row', 'col')
- value_grad: bfloat16 [32, 2048, 128], P('row', 'col')
- gate_grad: bfloat16 [32, 2048, 128], P('row', 'col')
- bias_grad: float32 [4, 2048, 2048], P(None, 'col', 'row')
Inputs may be any that keep to these rules, and one draw needn't show every extreme that they name: `block_mask`: every diagonal block is 1.
All inputs are finite; a program needn't handle non-finite values.
Results may differ from a plain program's by a relative error of at most 0.02.
Values may be sent and summed in bfloat16 or wider, within the bound.
No kernel may reach another device: no remote copies, remote signals or barrier semaphores. Data moves between devices by JAX's collectives and lax.ppermute only.
A program may use at most 64 MiB of HBM per device.

v0:
```python
import math
import jax
import jax.numpy as jnp
from jax import lax
from jax.sharding import PartitionSpec as P

H = 4
DH = 32
BLK = 128
NEGATIVE = -1000000000.0


def local(queries, keys, values, gate, bias, grad_out, block_mask):
    slab_rows, local_cols, channels = queries.shape
    head_count = H
    head_size = DH
    score_scale = 1.0 / math.sqrt(head_size)
    col_start = lax.axis_index("col") * local_cols
    kv_all = lax.all_gather(jnp.concatenate((keys, values), axis=2), "col", axis=1, tiled=True)
    key_all = kv_all[..., :channels]
    value_all = kv_all[..., channels:]
    all_cols = key_all.shape[1]
    query_heads = queries.reshape(slab_rows, local_cols, head_count, head_size)
    key_heads = key_all.reshape(slab_rows, all_cols, head_count, head_size)
    value_heads = value_all.reshape(slab_rows, all_cols, head_count, head_size)
    block_ids = (col_start + jnp.arange(local_cols, dtype=jnp.int32)) // BLK
    allowed = jnp.repeat(jnp.take(block_mask, block_ids, axis=0), BLK, axis=1) > 0
    products = jnp.einsum(
        "rjhd,rkhd->rhjk", query_heads, key_heads, preferred_element_type=jnp.float32
    )
    scores = products * score_scale + bias.astype(jnp.float32)[None]
    scores = jnp.where(allowed[None, None], scores, NEGATIVE)
    row_top = jnp.max(scores, axis=3, keepdims=True)
    log_total = row_top + jnp.log(jnp.sum(jnp.exp(scores - row_top), axis=3, keepdims=True))
    weights = jnp.exp(scores - log_total)
    probs = weights.astype(jnp.bfloat16)
    attended = jnp.einsum("rhjk,rkhd->rjhd", probs, value_heads, preferred_element_type=jnp.float32)
    gate_sig = jax.nn.sigmoid(gate.astype(jnp.float32)).reshape(
        slab_rows, local_cols, head_count, head_size
    )
    cotangent = grad_out.astype(jnp.float32).reshape(slab_rows, local_cols, head_count, head_size)
    gate_grad = (
        (cotangent * attended * gate_sig * (1.0 - gate_sig))
        .astype(jnp.bfloat16)
        .reshape(slab_rows, local_cols, channels)
    )
    out_grad = (cotangent * gate_sig).astype(jnp.bfloat16)
    grad_dot = jnp.transpose(jnp.sum(out_grad.astype(jnp.float32) * attended, axis=3), (0, 2, 1))
    prob_grad = jnp.einsum(
        "rjhd,rkhd->rhjk", out_grad, value_heads, preferred_element_type=jnp.float32
    )
    score_grad = weights * (prob_grad - grad_dot[..., None])
    score_grad_b = score_grad.astype(jnp.bfloat16)
    query_acc = jnp.einsum(
        "rhjk,rkhd->rjhd", score_grad_b, key_heads, preferred_element_type=jnp.float32
    )
    key_part = jnp.einsum(
        "rhjk,rjhd->rkhd", score_grad_b, query_heads, preferred_element_type=jnp.float32
    ).reshape(slab_rows, all_cols, channels)
    value_part = jnp.einsum(
        "rhjk,rjhd->rkhd", probs, out_grad, preferred_element_type=jnp.float32
    ).reshape(slab_rows, all_cols, channels)
    kv_part = jnp.concatenate((key_part, value_part), axis=2).astype(jnp.bfloat16)
    bias_part = jnp.sum(score_grad, axis=0).astype(jnp.bfloat16)
    col_count = all_cols // local_cols
    kv_moved = lax.all_to_all(
        kv_part.reshape(slab_rows, col_count, local_cols, 2 * channels), "col", 1, 1, tiled=True
    )
    kv_sum = jnp.sum(kv_moved.astype(jnp.float32), axis=1)
    key_grad = (kv_sum[..., :channels] * score_scale).astype(jnp.bfloat16)
    value_grad = kv_sum[..., channels:].astype(jnp.bfloat16)
    row_count = lax.axis_size("row")
    row_keys = all_cols // row_count
    bias_moved = lax.all_to_all(
        bias_part.reshape(head_count, local_cols, row_count, row_keys), "row", 2, 2, tiled=True
    )
    bias_grad = jnp.sum(bias_moved.astype(jnp.float32), axis=2)
    query_grad = (
        (query_acc * score_scale).astype(jnp.bfloat16).reshape(slab_rows, local_cols, channels)
    )
    return (query_grad, key_grad, value_grad, gate_grad, bias_grad)


def solution(mesh):
    return jax.shard_map(
        local,
        mesh=mesh,
        in_specs=(
            P("row", "col", None),
            P("row", "col", None),
            P("row", "col", None),
            P("row", "col", None),
            P(None, "col", None),
            P("row", "col", None),
            P(),
        ),
        out_specs=(
            P("row", "col", None),
            P("row", "col", None),
            P("row", "col", None),
            P("row", "col", None),
            P(None, "col", "row"),
        ),
        check_vma=False,
    )
```

profile of v0, /device:TPU:8, one launch (start us, length us, event | category | flops | bytes accessed | tf_op | source)
XLA Modules:
  0.0 172.1 jit_solution(1535113322949408808)
XLA Ops:
  7.2 0.0 copy-start
  7.2 0.0 copy-start.3
  7.2 0.0 all-gather.2.cloned.1.call-start
  7.2 1.5 pad_maximum_fusion.1
  8.8 0.0 all-gather.2.cloned.1.call-update
  8.8 0.9 copy.65
  9.8 0.9 add_divide_fusion
  10.6 0.1 copy.66
  10.7 4.1 %copy.64 = f32[4,128,2048]{1,2,0:T(8,128)} copy(bf16[4,128,2048]{2,1,0:T(8,128)(2,1)} %param.11) | data formatting | bytes 6291456 | tf_op jit(solution)/shard_map/convert_element_type | solution.py:31
  14.9 0.0 copy-done.3
  14.9 0.1 copy.63
  15.0 0.0 copy-done
  15.0 0.6 gather_fusion
  15.8 33.5 %all-gather.2.cloned.1.call-done = bf16[2,2048,256]{2,1,0:T(8,128)(2,1)} async-done(((bf16[2,128,256]{2,1,0:T(8,128)(2,1)}), bf16[2,2048,256]{2,1,0:T(8,128)(2,1)}) %all-gather.2.cloned.1.call-update) | async-done | bytes 2097168 | tf_op jit(solution)/shard_map/all_gather | solution.py:19
  49.3 1.7 fusion.15
  51.0 0.5 copy.61
  51.5 0.5 copy.67
  52.0 0.1 broadcast_in_dim.32
  52.1 4.5 %fusion.16 = (f32[2,4,128]{2,1,0:T(4,128)S(1)}, f32[2,4,128,2048]{2,3,1,0:T(8,128)S(1)}) fusion(f32[4,128,2048]{1,2,0:T(8,128)} %copy.64, bf16[2,2048,4,32]{1,3,2,0:T(8,128)(2,1)S(1)} %bitcast.49, bf16[2,128,4,32]{1,3,2,0:T(8,128)(2,1)S(1)} %bitcast.59, pred[128,2048]{0,1:T(8,128)(4,1)S(1)} %bitcast.58), kind=kOutput, calls=%fused_computation.42 | convolution fusion | flops 142605312 | bytes 13963264 | tf_op jit(solution)/shard_map/rjhd,rkhd->rhjk/dot_general | solution.py:28
  56.6 1.1 exponential_reduce_fusion
  57.7 1.7 %multiply_reduce_fusion = (f32[2,128,4]{1,2,0:T(4,128)S(1)}, bf16[2,128,4,32]{1,3,2,0:T(8,128)(2,1)S(1)}, bf16[2,128,4,32]{1,3,2,0:T(8,128)(2,1)S(1)}) fusion(f32[2,128,4,32]{1,3,2,0:T(8,128)S(1)} %bitcast.61, f32[2,128,4,32]{1,3,2,0:T(8,128)S(1)} %bitcast.62, bf16[2,2048,4,32]{1,3,2,0:T(8,128)(2,1)S(1)} %bitcast.51, ...), kind=kOutput, calls=%fused_computation.23 | convolution fusion | flops 138738688 | bytes 9838592 | tf_op jit(solution)/shard_map/rhjk,rkhd->rjhd/dot_general | solution.py:37
  59.5 1.5 convolution_convert_fusion
  61.0 5.0 %fusion.17 = (bf16[4,128,2048]{1,2,0:T(8,128)(2,1)}, bf16[2,4,128,2048]{2,3,1,0:T(8,128)(2,1)S(1)}) fusion(f32[2,4,128]{2,1,0:T(4,128)S(1)} %bitcast.70, bf16[2,128,4,32]{1,3,2,0:T(8,128)(2,1)S(1)} %get-tuple-element.26, bf16[2,2048,4,32]{1,3,2,0:T(8,128)(2,1)S(1)} %bitcast.52, f32[2,4,128,2048]{2,3,1,0:T(8,128)S(1)} %get-tuple-element.31, ...), kind=kOutput, calls=%fused_computation.43 | convolution fusion | flops 143654912 | bytes 15802368 | tf_op jit(solution)/shard_map/rjhd,rkhd->rhjk/dot_general | solution.py:49
  66.0 0.0 copy-start.1
  66.0 0.2 copy.88
  66.2 0.3 copy.74
  66.5 1.5 convolution_convert_fusion.1
  68.0 0.0 copy-done.1
  68.0 0.2 copy.87
  68.3 0.3 copy.73
  68.6 0.0 copy-start.2
  68.6 1.6 pad_maximum_fusion
  70.2 5.0 %all-to-all-start = ((bf16[2,16,128,256]{2,3,0,1:T(8,128)(2,1)}), bf16[2,16,128,256]{2,3,0,1:T(8,128)(2,1)}, u32[]{:S(2)}, u32[]{:S(2)}) async-start(bf16[2,16,128,256]{2,3,0,1:T(8,128)(2,1)} %pad_maximum_fusion), calls=%async_computation | async-start | bytes 4194304 | tf_op jit(solution)/shard_map/all_to_all | solution.py:66
  75.2 0.0 copy-done.2
  75.2 2.6 %copy.76 = bf16[4,128,16,128]{3,1,0,2:T(8,128)(2,1)} copy(bf16[4,128,16,128]{1,3,2,0:T(8,128)(2,1)S(1)} %bitcast.53) | data formatting | bytes 4194304 | tf_op jit(solution)/shard_map/convert_element_type | solution.py:64
  77.8 25.1 %all-to-all-done = bf16[2,16,128,256]{2,3,0,1:T(8,128)(2,1)} async-done(((bf16[2,16,128,256]{2,3,0,1:T(8,128)(2,1)}), bf16[2,16,128,256]{2,3,0,1:T(8,128)(2,1)}, u32[]{:S(2)}, u32[]{:S(2)}) %all-to-all-start) | async-done | bytes 2097184 | tf_op jit(solution)/shard_map/all_to_all | solution.py:66
  102.9 8.8 %all-to-all-start.1 = ((bf16[4,128,16,128]{3,1,0,2:T(8,128)(2,1)}), bf16[4,128,16,128]{3,1,0,2:T(8,128)(2,1)S(1)}, u32[]{:S(2)}, u32[]{:S(2)}) async-start(bf16[4,128,16,128]{3,1,0,2:T(8,128)(2,1)} %copy.76), calls=%async_computation.1 | async-start | bytes 4194304 | tf_op jit(solution)/shard_map/all_to_all | solution.py:74
  111.8 3.0 %fusion.8 = bf16[2,4,32,128]{3,2,1,0:T(8,128)(2,1)S(1)} fusion(bf16[2,2048,4,32]{1,3,2,0:T(8,128)(2,1)S(1)} %bitcast.50, bf16[2,4,128,2048]{2,3,1,0:T(8,128)(2,1)} %copy-done.1), kind=kOutput, calls=%fused_computation.17 | convolution fusion | flops 134283264 | bytes 5308416 | tf_op jit(solution)/shard_map/rhjk,rkhd->rjhd/dot_general | solution.py:54
  114.8 0.7 copy.77
  115.5 0.7 copy.80
  116.2 1.9 %convert_reduce_fusion.1 = f32[2,128,256]{1,2,0:T(8,128)S(1)} fusion(bf16[2,16,128,256]{2,3,0,1:T(8,128)(2,1)} %all-to-all-done), kind=kLoop, calls=%fused_computation.8 | loop fusion | flops 2031616 | bytes 2359296 | tf_op jit(solution)/shard_map/reduce_sum | solution.py:69
  118.2 0.7 copy.78
  118.9 0.7 copy.79
  119.7 44.5 %all-to-all-done.1 = bf16[4,128,16,128]{3,1,0,2:T(8,128)(2,1)S(1)} async-done(((bf16[4,128,16,128]{3,1,0,2:T(8,128)(2,1)}), bf16[4,128,16,128]{3,1,0,2:T(8,128)(2,1)S(1)}, u32[]{:S(2)}, u32[]{:S(2)}) %all-to-all-start.1) | async-done | bytes 2097184 | tf_op jit(solution)/shard_map/all_to_all | solution.py:74
  164.2 1.1 convert_reduce_fusion
  (8 shorter events, 0.1 us)
Async XLA Ops:
  7.2 7.9 %copy-start = (s32[16,16]{1,0:T(8,128)S(1)}, s32[16,16]{1,0:T(8,128)}, u32[]{:S(2)}) copy-start(s32[16,16]{1,0:T(8,128)} %param.13) | copy-start | bytes 3076
  7.2 7.7 %copy-start.3 = (bf16[2,128,128]{2,1,0:T(8,128)(2,1)S(1)}, bf16[2,128,128]{2,1,0:T(8,128)(2,1)}, u32[]{:S(2)}) copy-start(bf16[2,128,128]{2,1,0:T(8,128)(2,1)} %param.7) | copy-start | bytes 196612
  7.2 42.1 %all-gather.2.cloned.1.call-start = ((), (), s32[]{:S(2)}) async-start(), calls=%async_computation.2 | async-start | bytes 2228224 | tf_op jit(solution)/shard_map/all_gather | solution.py:19
  66.0 2.1 %copy-start.1 = (bf16[2,4,128,2048]{2,3,1,0:T(8,128)(2,1)}, bf16[2,4,128,2048]{2,3,1,0:T(8,128)(2,1)S(1)}, u32[]{:S(2)}) copy-start(bf16[2,4,128,2048]{2,3,1,0:T(8,128)(2,1)S(1)} %get-tuple-element.33) | copy-start | bytes 12582916
  68.6 6.6 %copy-start.2 = (bf16[4,128,2048]{1,2,0:T(8,128)(2,1)S(1)}, bf16[4,128,2048]{1,2,0:T(8,128)(2,1)}, u32[]{:S(2)}) copy-start(bf16[4,128,2048]{1,2,0:T(8,128)(2,1)} %get-tuple-element.32) | copy-start | bytes 6291460
  70.2 32.7 %all-to-all-start = ((bf16[2,16,128,256]{2,3,0,1:T(8,128)(2,1)}), bf16[2,16,128,256]{2,3,0,1:T(8,128)(2,1)}, u32[]{:S(2)}, u32[]{:S(2)}) async-start(bf16[2,16,128,256]{2,3,0,1:T(8,128)(2,1)} %pad_maximum_fusion), calls=%async_computation | async-start | bytes 4194304 | tf_op jit(solution)/shard_map/all_to_all | solution.py:66
  102.9 61.2 %all-to-all-start.1 = ((bf16[4,128,16,128]{3,1,0,2:T(8,128)(2,1)}), bf16[4,128,16,128]{3,1,0,2:T(8,128)(2,1)S(1)}, u32[]{:S(2)}, u32[]{:S(2)}) async-start(bf16[4,128,16,128]{3,1,0,2:T(8,128)(2,1)} %copy.76), calls=%async_computation.1 | async-start | bytes 4194304 | tf_op jit(solution)/shard_map/all_to_all | solution.py:74
Sparse Core Ops, SparseCore 0:
  10.4 38.8 all-gather.1
where the time goes:
time: 173 us; the launch traced here: 172 us
  waiting for transfers between devices  103 us (60%)
  matrix products  17.2 us (10%)
  local copies, waits for them, and re-layouts  15.4 us (9%)
  between operations  14.2 us (8%)
  starting transfers between devices  13.9 us (8%)
  other arithmetic  8.26 us (5%)
    all_to_all x1, waiting for transfers between devices, local(): lax.all_to_all(bias_part.reshape(head_count, local_cols, row_count, row_k...  44.5 us
    all_gather x1, waiting for transfers between devices, local(): lax.all_gather(jnp.concatenate((keys, values), axis=2), 'col', axis=1, ti...  33.5 us
    all_to_all x1, waiting for transfers between devices, local(): lax.all_to_all(kv_part.reshape(slab_rows, col_count, local_cols, 2 * chan...  25.1 us
    all_to_all x1, starting transfers between devices, local(): lax.all_to_all(bias_part.reshape(head_count, local_cols, row_count, row_k...  8.85 us
    all_to_all x1, starting transfers between devices, local(): lax.all_to_all(kv_part.reshape(slab_rows, col_count, local_cols, 2 * chan...  4.97 us
    dot_general x1, matrix products, local(): jnp.einsum('rjhd,rkhd->rhjk', out_grad, value_heads, preferred_element_ty...  4.96 us
    dot_general x1, matrix products, local(): jnp.einsum('rjhd,rkhd->rhjk', query_heads, key_heads, preferred_element_t...  4.46 us
    convert_element_type x1, local copies, waits for them, and re-layouts, local(): scores = products * score_scale + bias.astype(jnp.float32)[None]  4.13 us
  transfers between devices with their start and end apart: 3, of which 3 were waited for; matrix products, arithmetic and copies ran while one was open for 10% of the time, Pallas kernels for 0%

commit v1 on v0

--- a/solution.py
+++ b/solution.py
@@ -16,7 +16,12 @@
     head_size = DH
     score_scale = 1.0 / math.sqrt(head_size)
     col_start = lax.axis_index("col") * local_cols
-    kv_all = lax.all_gather(jnp.concatenate((keys, values), axis=2), "col", axis=1, tiled=True)
+    kv_all = jnp.concatenate(
+        lax.all_to_all(
+            jnp.stack([jnp.concatenate((keys, values), axis=2)] * lax.axis_size("col")), "col", 0, 0
+        ),
+        axis=1,
+    )
     key_all = kv_all[..., :channels]
     value_all = kv_all[..., channels:]
     all_cols = key_all.shape[1]

time: 173 us -> 157 us (0.908)
  between operations: 14.2 us -> 0.89 us
  waiting for transfers between devices: 103 us -> 91.9 us
  starting transfers between devices: 13.9 us -> 21 us
  local copies, waits for them, and re-layouts: 15.4 us -> 19.1 us
    all_gather x1 -> x0, waiting for transfers between devices: 33.5 us -> none  [local(): lax.all_gather(jnp.concatenate((keys, values), axis=2), 'col', axis=1, ti...]
    all_to_all x0 -> x1, waiting for transfers between devices: none -> 22.3 us  [local(): lax.all_to_all(jnp.stack([jnp.concatenate((keys, values), axis=2)] * lax....]
    all_to_all x0 -> x1, starting transfers between devices: none -> 5.77 us  [local(): lax.all_to_all(jnp.stack([jnp.concatenate((keys, values), axis=2)] * lax....]
    all_to_all x0 -> x1, local copies, waits for them, and re-layouts: none -> 2.6 us  [local(): lax.all_to_all(jnp.stack([jnp.concatenate((keys, values), axis=2)] * lax....]
    another operation x0 -> x1, local copies, waits for them, and re-layouts: none -> 1.81 us  [local(): jnp.stack([jnp.concatenate((keys, values), axis=2)] * lax.axis_size('col'))]
    unnamed x15 -> x19, local copies, waits for them, and re-layouts: 3.57 us -> 3.57 us
where the time goes in v1:
time: 157 us
  waiting for transfers between devices  91.9 us (59%)
  starting transfers between devices  21 us (13%)
  local copies, waits for them, and re-layouts  19.1 us (12%)
  matrix products  17.2 us (11%)
  other arithmetic  6.8 us (4%)
    all_to_all x1, waiting for transfers between devices, local(): lax.all_to_all(bias_part.reshape(head_count, local_cols, row_count, row_k...  44.5 us
    all_to_all x1, waiting for transfers between devices, local(): lax.all_to_all(kv_part.reshape(slab_rows, col_count, local_cols, 2 * chan...  25.1 us
    all_to_all x1, waiting for transfers between devices, local(): lax.all_to_all(jnp.stack([jnp.concatenate((keys, values), axis=2)] * lax....  22.3 us
    all_to_all x1, starting transfers between devices, local(): lax.all_to_all(bias_part.reshape(head_count, local_cols, row_count, row_k...  10.3 us
    all_to_all x1, starting transfers between devices, local(): lax.all_to_all(jnp.stack([jnp.concatenate((keys, values), axis=2)] * lax....  5.77 us
    all_to_all x1, starting transfers between devices, local(): lax.all_to_all(kv_part.reshape(slab_rows, col_count, local_cols, 2 * chan...  4.97 us
    dot_general x1, matrix products, local(): jnp.einsum('rjhd,rkhd->rhjk', out_grad, value_heads, preferred_element_ty...  4.97 us
    dot_general x1, matrix products, local(): jnp.einsum('rjhd,rkhd->rhjk', query_heads, key_heads, preferred_element_t...  4.46 us
  transfers between devices with their start and end apart: 3, of which 3 were waited for; matrix products, arithmetic and copies ran while one was open for 10% of the time, Pallas kernels for 0%

profile of v1, /device:TPU:8, one launch (start us, length us, event | category | flops | bytes accessed | tf_op | source)
XLA Modules:
  0.0 157.0 jit_solution(14494070827637920644)
XLA Ops:
  0.6 0.0 copy-start
  0.6 0.0 copy-start.3
  0.7 0.0 copy-start.4
  0.7 0.9 pad_maximum_fusion.1
  1.6 0.1 copy.80
  1.7 1.8 %stack.2 = bf16[16,2,128,256]{2,3,1,0:T(8,128)(2,1)} broadcast(bf16[2,128,256]{1,2,0:T(8,128)(2,1)S(1)} %copy.80), dimensions={1,2,3} | broadcast | bytes 2228224 | tf_op jit(solution)/shard_map/stack | solution.py:21
  3.5 5.8 %all-to-all-start = ((bf16[16,2,128,256]{2,3,1,0:T(8,128)(2,1)}), bf16[16,2,128,256]{2,3,1,0:T(8,128)(2,1)S(1)}, u32[]{:S(2)}, u32[]{:S(2)}) async-start(bf16[16,2,128,256]{2,3,1,0:T(8,128)(2,1)} %stack.2), calls=%async_computation | async-start | bytes 4194304 | tf_op jit(solution)/shard_map/all_to_all | solution.py:20
  9.3 0.0 copy-start.5
  9.3 0.0 copy-done.3
  9.3 0.1 copy.86
  9.4 0.0 copy-done.4
  9.5 0.1 copy.87
  9.6 4.1 %copy.85 = f32[4,128,2048]{1,2,0:T(8,128)} copy(bf16[4,128,2048]{2,1,0:T(8,128)(2,1)} %param.11) | data formatting | bytes 6291456 | tf_op jit(solution)/shard_map/convert_element_type | solution.py:36
  13.7 0.0 copy-done.5
  13.7 0.1 copy.84
  13.9 0.0 copy-done
  13.9 0.6 gather_fusion
  14.6 22.3 %all-to-all-done = bf16[16,2,128,256]{2,3,1,0:T(8,128)(2,1)S(1)} async-done(((bf16[16,2,128,256]{2,3,1,0:T(8,128)(2,1)}), bf16[16,2,128,256]{2,3,1,0:T(8,128)(2,1)S(1)}, u32[]{:S(2)}, u32[]{:S(2)}) %all-to-all-start) | async-done | bytes 2097184 | tf_op jit(solution)/shard_map/all_to_all | solution.py:20
  36.9 2.6 %copy.81 = bf16[16,2,128,256]{3,2,0,1:T(8,128)(2,1)} copy(bf16[16,2,128,256]{2,3,1,0:T(8,128)(2,1)S(1)} %all-to-all-done) | data formatting | bytes 4194304 | tf_op jit(solution)/shard_map/all_to_all | solution.py:20
  39.6 1.7 %fusion.15 = (bf16[2,2048,128]{2,1,0:T(8,128)(2,1)S(1)}, bf16[2,2048,128]{2,1,0:T(8,128)(2,1)S(1)}) fusion(bf16[2,2048,256]{2,1,0:T(8,128)(2,1)} %bitcast.57), kind=kLoop, calls=%fused_computation.41 | loop fusion | bytes 4194304 | tf_op jit(solution)/shard_map/slice | solution.py:26
  41.3 0.5 copy.82
  41.8 0.5 copy.88
  42.3 0.1 broadcast_in_dim.32
  42.4 4.5 %fusion.16 = (f32[2,4,128]{2,1,0:T(4,128)S(1)}, f32[2,4,128,2048]{2,3,1,0:T(8,128)S(1)}) fusion(f32[4,128,2048]{1,2,0:T(8,128)} %copy.85, bf16[2,2048,4,32]{1,3,2,0:T(8,128)(2,1)S(1)} %bitcast.52, bf16[2,128,4,32]{1,3,2,0:T(8,128)(2,1)S(1)} %bitcast.63, pred[128,2048]{0,1:T(8,128)(4,1)S(1)} %bitcast.62), kind=kOutput, calls=%fused_computation.42 | convolution fusion | flops 142605312 | bytes 13963264 | tf_op jit(solution)/shard_map/rjhd,rkhd->rhjk/dot_general | solution.py:33
  46.9 1.1 exponential_reduce_fusion
  48.0 1.7 %multiply_reduce_fusion = (f32[2,128,4]{1,2,0:T(4,128)S(1)}, bf16[2,128,4,32]{1,3,2,0:T(8,128)(2,1)S(1)}, bf16[2,128,4,32]{1,3,2,0:T(8,128)(2,1)S(1)}) fusion(f32[2,128,4,32]{1,3,2,0:T(8,128)S(1)} %bitcast.65, f32[2,128,4,32]{1,3,2,0:T(8,128)S(1)} %bitcast.66, bf16[2,2048,4,32]{1,3,2,0:T(8,128)(2,1)S(1)} %bitcast.54, ...), kind=kOutput, calls=%fused_computation.23 | convolution fusion | flops 138738688 | bytes 9838592 | tf_op jit(solution)/shard_map/rhjk,rkhd->rjhd/dot_general | solution.py:42
  49.8 1.5 convolution_convert_fusion
  51.3 5.0 %fusion.17 = (bf16[4,128,2048]{1,2,0:T(8,128)(2,1)}, bf16[2,4,128,2048]{2,3,1,0:T(8,128)(2,1)S(1)}) fusion(f32[2,4,128]{2,1,0:T(4,128)S(1)} %bitcast.74, bf16[2,128,4,32]{1,3,2,0:T(8,128)(2,1)S(1)} %get-tuple-element.31, bf16[2,2048,4,32]{1,3,2,0:T(8,128)(2,1)S(1)} %bitcast.55, f32[2,4,128,2048]{2,3,1,0:T(8,128)S(1)} %get-tuple-element.36, ...), kind=kOutput, calls=%fused_computation.43 | convolution fusion | flops 143654912 | bytes 15802368 | tf_op jit(solution)/shard_map/rjhd,rkhd->rhjk/dot_general | solution.py:54
  56.3 0.0 copy-start.1
  56.3 0.2 copy.109
  56.5 0.3 copy.95
  56.8 1.5 convolution_convert_fusion.1
  58.3 0.0 copy-done.1
  58.3 0.2 copy.108
  58.6 0.3 copy.94
  58.8 0.0 copy-start.2
  58.9 1.6 %pad_maximum_fusion = bf16[2,16,128,256]{2,3,0,1:T(8,128)(2,1)} fusion(bf16[2,16,128,128]{2,3,0,1:T(8,128)(2,1)S(1)} %copy.95, bf16[2,16,128,128]{2,3,0,1:T(8,128)(2,1)S(1)} %copy.94), kind=kLoop, calls=%fused_computation.11 | loop fusion | flops 4194304 | bytes 4194304 | tf_op jit(solution)/shard_map/concatenate | solution.py:68
  60.5 5.0 %all-to-all-start.1 = ((bf16[2,16,128,256]{2,3,0,1:T(8,128)(2,1)}), bf16[2,16,128,256]{2,3,0,1:T(8,128)(2,1)}, u32[]{:S(2)}, u32[]{:S(2)}) async-start(bf16[2,16,128,256]{2,3,0,1:T(8,128)(2,1)} %pad_maximum_fusion), calls=%async_computation.1 | async-start | bytes 4194304 | tf_op jit(solution)/shard_map/all_to_all | solution.py:71
  65.4 0.0 copy-done.2
  65.5 2.6 %copy.97 = bf16[4,128,16,128]{3,1,0,2:T(8,128)(2,1)} copy(bf16[4,128,16,128]{1,3,2,0:T(8,128)(2,1)S(1)} %bitcast.56) | data formatting | bytes 4194304 | tf_op jit(solution)/shard_map/convert_element_type | solution.py:69
  68.1 25.1 %all-to-all-done.1 = bf16[2,16,128,256]{2,3,0,1:T(8,128)(2,1)} async-done(((bf16[2,16,128,256]{2,3,0,1:T(8,128)(2,1)}), bf16[2,16,128,256]{2,3,0,1:T(8,128)(2,1)}, u32[]{:S(2)}, u32[]{:S(2)}) %all-to-all-start.1) | async-done | bytes 2097184 | tf_op jit(solution)/shard_map/all_to_all | solution.py:71
  93.2 10.3 %all-to-all-start.2 = ((bf16[4,128,16,128]{3,1,0,2:T(8,128)(2,1)}), bf16[4,128,16,128]{3,1,0,2:T(8,128)(2,1)S(1)}, u32[]{:S(2)}, u32[]{:S(2)}) async-start(bf16[4,128,16,128]{3,1,0,2:T(8,128)(2,1)} %copy.97), calls=%async_computation.2 | async-start | bytes 4194304 | tf_op jit(solution)/shard_map/all_to_all | solution.py:79
  103.5 3.0 %fusion.8 = bf16[2,4,32,128]{3,2,1,0:T(8,128)(2,1)S(1)} fusion(bf16[2,2048,4,32]{1,3,2,0:T(8,128)(2,1)S(1)} %bitcast.53, bf16[2,4,128,2048]{2,3,1,0:T(8,128)(2,1)} %copy-done.1), kind=kOutput, calls=%fused_computation.17 | convolution fusion | flops 134283264 | bytes 5308416 | tf_op jit(solution)/shard_map/rhjk,rkhd->rjhd/dot_general | solution.py:59
  106.5 0.7 copy.98
  107.2 0.7 copy.101
  108.0 1.9 %convert_reduce_fusion.1 = f32[2,128,256]{1,2,0:T(8,128)S(1)} fusion(bf16[2,16,128,256]{2,3,0,1:T(8,128)(2,1)} %all-to-all-done.1), kind=kLoop, calls=%fused_computation.8 | loop fusion | flops 2031616 | bytes 2359296 | tf_op jit(solution)/shard_map/reduce_sum | solution.py:74
  109.9 0.7 copy.99
  110.7 0.7 copy.100
  111.4 44.5 %all-to-all-done.2 = bf16[4,128,16,128]{3,1,0,2:T(8,128)(2,1)S(1)} async-done(((bf16[4,128,16,128]{3,1,0,2:T(8,128)(2,1)}), bf16[4,128,16,128]{3,1,0,2:T(8,128)(2,1)S(1)}, u32[]{:S(2)}, u32[]{:S(2)}) %all-to-all-start.2) | async-done | bytes 2097184 | tf_op jit(solution)/shard_map/all_to_all | solution.py:79
  155.9 1.1 convert_reduce_fusion
  (9 shorter events, 0.2 us)
Async XLA Ops:
  0.6 13.3 %copy-start = (s32[16,16]{1,0:T(8,128)S(1)}, s32[16,16]{1,0:T(8,128)}, u32[]{:S(2)}) copy-start(s32[16,16]{1,0:T(8,128)} %param.13) | copy-start | bytes 3076
  0.6 8.7 %copy-start.3 = (bf16[2,128,128]{2,1,0:T(8,128)(2,1)S(1)}, bf16[2,128,128]{2,1,0:T(8,128)(2,1)}, u32[]{:S(2)}) copy-start(bf16[2,128,128]{2,1,0:T(8,128)(2,1)} %param.12) | copy-start | bytes 196612
  0.7 8.8 %copy-start.4 = (bf16[2,128,128]{2,1,0:T(8,128)(2,1)S(1)}, bf16[2,128,128]{2,1,0:T(8,128)(2,1)}, u32[]{:S(2)}) copy-start(bf16[2,128,128]{2,1,0:T(8,128)(2,1)} %param.10) | copy-start | bytes 196612
  3.5 33.4 %all-to-all-start = ((bf16[16,2,128,256]{2,3,1,0:T(8,128)(2,1)}), bf16[16,2,128,256]{2,3,1,0:T(8,128)(2,1)S(1)}, u32[]{:S(2)}, u32[]{:S(2)}) async-start(bf16[16,2,128,256]{2,3,1,0:T(8,128)(2,1)} %stack.2), calls=%async_computation | async-start | bytes 4194304 | tf_op jit(solution)/shard_map/all_to_all | solution.py:20
  9.3 4.4 %copy-start.5 = (bf16[2,128,128]{2,1,0:T(8,128)(2,1)S(1)}, bf16[2,128,128]{2,1,0:T(8,128)(2,1)}, u32[]{:S(2)}) copy-start(bf16[2,128,128]{2,1,0:T(8,128)(2,1)} %param.7) | copy-start | bytes 196612
  56.3 2.1 %copy-start.1 = (bf16[2,4,128,2048]{2,3,1,0:T(8,128)(2,1)}, bf16[2,4,128,2048]{2,3,1,0:T(8,128)(2,1)S(1)}, u32[]{:S(2)}) copy-start(bf16[2,4,128,2048]{2,3,1,0:T(8,128)(2,1)S(1)} %get-tuple-element.38) | copy-start | bytes 12582916
  58.8 6.6 %copy-start.2 = (bf16[4,128,2048]{1,2,0:T(8,128)(2,1)S(1)}, bf16[4,128,2048]{1,2,0:T(8,128)(2,1)}, u32[]{:S(2)}) copy-start(bf16[4,128,2048]{1,2,0:T(8,128)(2,1)} %get-tuple-element.37) | copy-start | bytes 6291460
  60.5 32.7 %all-to-all-start.1 = ((bf16[2,16,128,256]{2,3,0,1:T(8,128)(2,1)}), bf16[2,16,128,256]{2,3,0,1:T(8,128)(2,1)}, u32[]{:S(2)}, u32[]{:S(2)}) async-start(bf16[2,16,128,256]{2,3,0,1:T(8,128)(2,1)} %pad_maximum_fusion), calls=%async_computation.1 | async-start | bytes 4194304 | tf_op jit(solution)/shard_map/all_to_all | solution.py:71
  93.2 62.7 %all-to-all-start.2 = ((bf16[4,128,16,128]{3,1,0,2:T(8,128)(2,1)}), bf16[4,128,16,128]{3,1,0,2:T(8,128)(2,1)S(1)}, u32[]{:S(2)}, u32[]{:S(2)}) async-start(bf16[4,128,16,128]{3,1,0,2:T(8,128)(2,1)} %copy.97), calls=%async_computation.2 | async-start | bytes 4194304 | tf_op jit(solution)/shard_map/all_to_all | solution.py:79
